TPU v7x, 256 devices: a whole 4x4x8 slice. The times are simulated.
256 devices in a mesh: seq: 32 (over z, y_lo, core), tp: 8 (over y_hi, x).
Axes of the slice: x: 4, y: 4 (y_hi: 2, y_lo: 2; y = y_hi * 2 + y_lo), z: 8, core: 2. Of those that a mesh axis runs over, the one named last changes fastest.
Arguments:
- qkv_se: bfloat16 [16384, 3, 4096], P('seq', None, 'tp'), may hold values from -6 to 6
- residual: bfloat16 [16384, 4096], P('seq', 'tp'), may hold values from -108 to 108
- taps_se: bfloat16 [256, 7], P('tp'), may hold values from -2 to 2
- skip_se: bfloat16 [4096], P('tp'), may hold values from 0.5 to 1.5
- w_out: bfloat16 [4096, 4096], P('tp', 'seq'), may hold values from -0.1875 to 0.1875
- norm_gain: bfloat16 [4096], replicated, may hold values from 0.5 to 1.5
- w_in: bfloat16 [4096, 3, 4096], P('seq', None, 'tp'), may hold values from -0.09375 to 0.09375
- taps_mr: bfloat16 [256, 128], P('tp'), may hold values from -0.5 to 0.5
- skip_mr: bfloat16 [4096], P('tp'), may hold values from 0.5 to 1.5
Outputs:
- mixed: bfloat16 [16384, 4096], P('seq', 'tp')
All inputs are finite; a program needn't handle non-finite values.
Results may differ from a plain program's by a relative error of at most 0.0085.
Values may be sent and summed in bfloat16 or wider, within the bound.
No kernel may reach another device: no remote copies, remote signals or barrier semaphores. Data moves between devices by JAX's collectives and lax.ppermute only.
A program may use at most 64 MiB of HBM per device.

v0:
```python
import jax
import jax.numpy as jnp
from jax import lax
from jax.sharding import PartitionSpec as P

GROUP = 16
SE_TAPS = 7
MR_TAPS = 128
norm_eps = 1e-05


def shifted(block, axis, distance):
    devices = range(lax.axis_size(axis))
    route = [(i - distance, i) for i in devices if i - distance in devices]
    return lax.ppermute(block, axis, route)


def toeplitz_pair(taps):
    offsets = lax.broadcasted_iota(jnp.int32, (MR_TAPS, MR_TAPS), 0) - lax.broadcasted_iota(
        jnp.int32, (MR_TAPS, MR_TAPS), 1
    )
    lag_ids = lax.broadcasted_iota(jnp.int32, (MR_TAPS, MR_TAPS, MR_TAPS), 0)
    picks = (jnp.remainder(offsets, MR_TAPS)[None] == lag_ids).astype(jnp.bfloat16)
    table = jnp.einsum("gj,jts->gts", taps, picks, preferred_element_type=jnp.float32).astype(
        jnp.bfloat16
    )
    lower = jnp.where(offsets[None] >= 0, table, jnp.zeros_like(table))
    upper = jnp.where(offsets[None] < 0, table, jnp.zeros_like(table))
    return (lower, upper)


def project_out(y_se, w_out):
    return jnp.dot(
        y_se, lax.all_gather(w_out, "seq", axis=1, tiled=True), preferred_element_type=jnp.float32
    )


def per_device(qkv_se, residual, taps_se, skip_se, w_out, norm_gain, w_in, taps_mr, skip_mr):
    row_count = qkv_se.shape[0]
    chan_width = qkv_se.shape[2]
    local_groups = chan_width // GROUP
    query_se = qkv_se[:, 0].astype(jnp.float32)
    u_se = (qkv_se[:, 1].astype(jnp.float32) * qkv_se[:, 2].astype(jnp.float32)).astype(
        jnp.bfloat16
    )
    incoming_se = shifted(u_se[row_count - (SE_TAPS - 1) :], "seq", 1)
    extended = jnp.concatenate([incoming_se, u_se], axis=0).astype(jnp.float32)
    per_channel = jnp.repeat(taps_se.astype(jnp.float32), GROUP, axis=0)
    conv_se = jnp.zeros((row_count, chan_width), jnp.float32)
    for tap_index in range(SE_TAPS):
        begin = SE_TAPS - 1 - tap_index
        conv_se = conv_se + per_channel[:, tap_index] * extended[begin : begin + row_count]
    y_se = (query_se * (conv_se + skip_se.astype(jnp.float32) * u_se.astype(jnp.float32))).astype(
        jnp.bfloat16
    )
    gain_full = norm_gain.astype(jnp.float32)
    partial_out = project_out(y_se, w_out)
    share = lax.psum_scatter(partial_out, "tp", scatter_dimension=1, tiled=True)
    stream = residual.astype(jnp.float32) + share
    squares = lax.psum(jnp.sum(stream * stream, axis=1), "tp")
    scale = lax.rsqrt(squares / (chan_width * lax.axis_size("tp")) + norm_eps)
    my_gain = lax.dynamic_slice_in_dim(gain_full, lax.axis_index("tp") * chan_width, chan_width, 0)
    normed = (stream * scale[:, None] * my_gain).astype(jnp.bfloat16)
    gathered = lax.all_gather(normed, "tp", axis=1, tiled=True)
    piece = lax.all_gather(w_in, "seq", axis=0, tiled=True)
    flat_piece = piece.reshape(piece.shape[0], 3 * chan_width)
    proj = jnp.dot(gathered, flat_piece, preferred_element_type=jnp.float32).reshape(
        row_count, 3, chan_width
    )
    query_mr = proj[:, 0]
    u_mr = (proj[:, 1] * proj[:, 2]).astype(jnp.bfloat16)
    lower, upper = toeplitz_pair(taps_mr)
    block_count = row_count // MR_TAPS
    blocks = u_mr.reshape(block_count, MR_TAPS, local_groups, GROUP)
    inside = jnp.einsum("gts,bsgc->btgc", lower, blocks, preferred_element_type=jnp.float32)
    tail_rows = shifted(blocks[block_count - 1], "seq", 1)
    earlier = jnp.concatenate([tail_rows[None], blocks[: block_count - 1]], axis=0)
    conv_mr = inside + jnp.einsum(
        "gts,bsgc->btgc", upper, earlier, preferred_element_type=jnp.float32
    )
    conv_mr = conv_mr.reshape(row_count, chan_width)
    return (query_mr * (conv_mr + skip_mr.astype(jnp.float32) * u_mr.astype(jnp.float32))).astype(
        jnp.bfloat16
    )


def solution(mesh):
    placed = (
        P("seq", None, "tp"),
        P("seq", "tp"),
        P("tp", None),
        P("tp"),
        P("tp", "seq"),
        P(),
        P("seq", None, "tp"),
        P("tp", None),
        P("tp"),
    )
    return jax.shard_map(
        per_device, mesh=mesh, in_specs=placed, out_specs=P("seq", "tp"), check_vma=False
    )
```

profile of v0, /device:TPU:105, one launch (start us, length us, event | category | flops | bytes accessed | tf_op | source)
XLA Modules:
  0.0 438.2 jit_solution(15193154201921998345)
XLA Ops:
  6.5 0.0 copy-start
  6.5 0.0 copy-start.3
  6.5 0.0 all-gather.4.cloned.1.call-start
  6.5 0.7 all-gather.4.cloned.1.call-update
  7.3 0.0 reduce-scatter.2.cloned.1.call-start
  7.3 1.3 multiply_convert_fusion.1
  8.7 5.2 %collective-permute-start = (bf16[6,512]{1,0:T(8,128)(2,1)S(1)}, bf16[6,512]{1,0:T(8,128)(2,1)S(1)}, u32[]{:S(2)}, u32[]{:S(2)}) collective-permute-start(bf16[6,512]{1,0:T(8,128)(2,1)S(1)} %slice_bitcast_fusion.1), channel_id=1, source_target_pairs={{0,8},{8,16},{16,24},{24,32},{32,40},{40,48},{48,56},{56,64},{64,7... | collective-permute-start | bytes 18440 | tf_op jit(solution)/shard_map/ppermute | solution.py:15
  13.9 0.8 broadcast_in_dim.26
  14.6 0.1 reshape.75
  14.8 1.3 fusion.51
  16.1 0.0 copy-done.3
  16.1 0.0 collective-permute-done
  16.1 0.2 maximum_convert_fusion
  16.3 65.7 %all-gather.4.cloned.1.call-done = bf16[512,4096]{1,0:T(8,128)(2,1)} async-done(((bf16[512,128]{1,0:T(8,128)(2,1)}), bf16[512,4096]{1,0:T(8,128)(2,1)}) %all-gather.4.cloned.1.call-update) | async-done | bytes 4194320 | tf_op jit(solution)/shard_map/all_gather | solution.py:34
  82.0 8.7 %fusion.22 = f32[512,4096]{1,0:T(8,128)} fusion(bf16[512,4096]{1,0:T(8,128)(2,1)} %all-gather.4.cloned.1.call-done, f32[518,512]{1,0:T(8,128)S(1)} %maximum_convert_fusion, f32[512]{0:T(512)S(1)} %convert_element_type.78, f32[512]{0:T(512)S(1)} %bitcast.74, f32[512]{0:T(512)S(1)} %bitcast.75, f32[512]{0:T(512)S(1)} %bitcast.76, f32[512]{0:T(512)S(1)} %bitcast.77, ...), kind=kOutput, calls=%fused_computation.42 | convolution fusion | flops 2152464384 | bytes 20987904 | tf_op jit(solution)/shard_map/dot_general | solution.py:33
  90.7 0.0 copy-start.2
  90.7 0.0 copy-start.1
  90.7 0.0 reduce-scatter.2.cloned.1.call-update
  90.8 0.0 copy-start.4
  90.8 0.0 all-gather.8.cloned.1.call-start
  90.8 0.9 copy-done.2
  91.7 0.9 copy.24
  92.7 0.0 all-gather.8.cloned.1.call-update
  92.7 0.0 all-gather.6.cloned.1.call-start
  92.8 0.8 dynamic-slice_convert_fusion
  93.5 115.5 %reduce-scatter.2.cloned.1.call-done = f32[512,512]{1,0:T(8,128)} async-done(((f32[512,4096]{1,0:T(8,128)}), f32[512,512]{1,0:T(8,128)}) %reduce-scatter.2.cloned.1.call-update) | async-done | bytes 1048592 | tf_op jit(solution)/shard_map/reduce_scatter | solution.py:58
  209.0 0.0 copy-done.1
  209.1 1.4 multiply_reduce_fusion
  210.5 16.9 %psum.7 = f32[512]{0:T(512)S(1)} all-reduce(f32[512]{0:T(512)S(1)} %multiply_reduce_fusion), channel_id=1, replica_groups=mesh['seq'=32,'tp'=8] {'tp'}, use_global_device_ids=true, to_apply=%region_2.0 | all-reduce | flops 512 | bytes 4096 | tf_op jit(solution)/shard_map/psum | solution.py:60
  227.4 2.3 multiply_convert_fusion
  229.7 0.0 all-gather.6.cloned.1.call-update
  229.7 0.0 copy-done.4
  229.8 0.0 copy-done
  229.8 3.3 select_bitcast_fusion
  233.1 83.3 %all-gather.8.cloned.1.call-done = bf16[4096,3,512]{0,2,1:T(8,128)(2,1)} async-done(((bf16[128,3,512]{0,2,1:T(8,128)(2,1)}), bf16[4096,3,512]{0,2,1:T(8,128)(2,1)}) %all-gather.8.cloned.1.call-update) | async-done | bytes 12582928 | tf_op jit(solution)/shard_map/all_gather | solution.py:65
  316.4 81.6 %all-gather.6.cloned.1.call-done = bf16[512,4096]{1,0:T(8,128)(2,1)} async-done(((bf16[512,512]{1,0:T(8,128)(2,1)}), bf16[512,4096]{1,0:T(8,128)(2,1)}) %all-gather.6.cloned.1.call-update) | async-done | bytes 4194320 | tf_op jit(solution)/shard_map/all_gather | solution.py:64
  398.0 10.6 %fusion = f32[512,3,512]{0,2,1:T(8,128)S(1)} fusion(bf16[4096,3,512]{0,2,1:T(8,128)(2,1)} %all-gather.8.cloned.1.call-done, bf16[512,4096]{1,0:T(8,128)(2,1)} %all-gather.6.cloned.1.call-done), kind=kOutput, calls=%fused_computation | convolution fusion | flops 6442450944 | bytes 19922944 | tf_op jit(solution)/shard_map/dot_general | solution.py:67
  408.7 0.9 fusion.9
  409.6 0.0 slice-start
  409.6 2.1 convert_element_type.84
  411.7 1.6 slice.121
  413.2 7.2 %collective-permute-start.1 = (bf16[128,32,16]{0,2,1:T(8,128)(2,1)}, bf16[128,32,16]{0,2,1:T(8,128)(2,1)}, u32[]{:S(2)}, u32[]{:S(2)}) collective-permute-start(bf16[128,32,16]{0,2,1:T(8,128)(2,1)} %bitcast.18), channel_id=1, source_target_pairs={{0,8},{8,16},{16,24},{24,32},{32,40},{40,48},{48,56},{56,64},{64,7... | collective-permute-start | bytes 393224 | tf_op jit(solution)/shard_map/ppermute | solution.py:15
  420.4 3.2 fusion.20
  423.6 0.0 slice-done
  423.6 0.9 slice.102
  424.5 1.1 copy.27
  425.6 0.0 collective-permute-done.1
  425.7 2.5 fusion.6
  428.1 0.4 copy.29
  428.6 1.0 fusion.8
  429.6 2.0 copy.30
  (7 shorter events, 0.1 us)
Async XLA Ops:
  6.5 223.3 %copy-start = (bf16[32,128]{1,0:T(8,128)(2,1)S(1)}, bf16[32,128]{1,0:T(8,128)(2,1)}, u32[]{:S(2)}) copy-start(bf16[32,128]{1,0:T(8,128)(2,1)} %param.16) | copy-start | bytes 24580
  6.5 9.6 %copy-start.3 = (bf16[512]{0:T(512)(128)(2,1)S(1)}, bf16[512]{0:T(512)(128)(2,1)}, u32[]{:S(2)}) copy-start(bf16[512]{0:T(512)(128)(2,1)} %param.12) | copy-start | bytes 3076
  6.5 75.5 %all-gather.4.cloned.1.call-start = ((), (), s32[]{:S(2)}) async-start(), calls=%async_computation.1 | async-start | bytes 4325376 | tf_op jit(solution)/shard_map/all_gather | solution.py:34
  7.3 201.8 %reduce-scatter.2.cloned.1.call-start = ((), (), s32[]{:S(2)}) async-start(), calls=%async_computation.2 | async-start | bytes 9437184 | tf_op jit(solution)/shard_map/reduce_scatter | solution.py:58
  8.7 7.5 %collective-permute-start = (bf16[6,512]{1,0:T(8,128)(2,1)S(1)}, bf16[6,512]{1,0:T(8,128)(2,1)S(1)}, u32[]{:S(2)}, u32[]{:S(2)}) collective-permute-start(bf16[6,512]{1,0:T(8,128)(2,1)S(1)} %slice_bitcast_fusion.1), channel_id=1, source_target_pairs={{0,8},{8,16},{16,24},{24,32},{32,40},{40,48},{48,56},{56,64},{64,7... | collective-permute-start | bytes 18440 | tf_op jit(solution)/shard_map/ppermute | solution.py:15
  90.7 1.0 copy-start.2
  90.7 118.3 %copy-start.1 = (bf16[512,512]{1,0:T(8,128)(2,1)S(1)}, bf16[512,512]{1,0:T(8,128)(2,1)}, u32[]{:S(2)}) copy-start(bf16[512,512]{1,0:T(8,128)(2,1)} %param.10) | copy-start | bytes 1572868
  90.8 138.9 %copy-start.4 = (bf16[512]{0:T(512)(128)(2,1)S(1)}, bf16[512]{0:T(512)(128)(2,1)}, u32[]{:S(2)}) copy-start(bf16[512]{0:T(512)(128)(2,1)} %param.17) | copy-start | bytes 3076
  90.8 225.7 %all-gather.8.cloned.1.call-start = ((), (), s32[]{:S(2)}) async-start(), calls=%async_computation.4 | async-start | bytes 12976128 | tf_op jit(solution)/shard_map/all_gather | solution.py:65
  92.7 305.3 %all-gather.6.cloned.1.call-start = ((), (), s32[]{:S(2)}) async-start(), calls=%async_computation.3 | async-start | bytes 4718592 | tf_op jit(solution)/shard_map/all_gather | solution.py:64
  409.6 14.0 %slice-start = ((bf16[512,1,512]{0,2,1:T(8,128)(2,1)}), bf16[384,1,512]{0,2,1:T(8,128)(2,1)S(1)}, s32[]{:S(2)}) async-start(bf16[512,1,512]{0,2,1:T(8,128)(2,1)} %fusion.9), calls=%async_computation.5 | async-start | bytes 786432 | tf_op jit(solution)/shard_map/slice | solution.py:77
  413.2 12.4 %collective-permute-start.1 = (bf16[128,32,16]{0,2,1:T(8,128)(2,1)}, bf16[128,32,16]{0,2,1:T(8,128)(2,1)}, u32[]{:S(2)}, u32[]{:S(2)}) collective-permute-start(bf16[128,32,16]{0,2,1:T(8,128)(2,1)} %bitcast.18), channel_id=1, source_target_pairs={{0,8},{8,16},{16,24},{24,32},{32,40},{40,48},{48,56},{56,64},{64,7... | collective-permute-start | bytes 393224 | tf_op jit(solution)/shard_map/ppermute | solution.py:15
Sparse Core Ops, SparseCore 0:
  9.1 72.8 all-gather.3
  90.9 118.1 reduce-scatter.1
  210.8 105.5 all-gather.7
  318.8 79.2 all-gather.5
where the time goes:
time: 439 us; the launch traced here: 438 us
  waiting for transfers between devices  347 us (79%)
  matrix products  28.3 us (6%)
  blocking collectives  16.9 us (4%)
  between operations  13.3 us (3%)
  starting transfers between devices  12.5 us (3%)
  local copies, waits for them, and re-layouts  10.9 us (2%)
  other arithmetic  9.38 us (2%)
    reduce_scatter x1, waiting for transfers between devices, per_device(): share = lax.psum_scatter(partial_out, 'tp', scatter_dimension=1, tiled=True)  116 us
    all_gather x1, waiting for transfers between devices, per_device(): piece = lax.all_gather(w_in, 'seq', axis=0, tiled=True)  83.3 us
    all_gather x1, waiting for transfers between devices, per_device(): gathered = lax.all_gather(normed, 'tp', axis=1, tiled=True)  81.6 us
    all_gather x1, waiting for transfers between devices, project_out(): lax.all_gather(w_out, 'seq', axis=1, tiled=True)  65.7 us
    psum x1, blocking collectives, per_device(): squares = lax.psum(jnp.sum(stream * stream, axis=1), 'tp')  16.9 us
    ppermute x2, starting transfers between devices, shifted(): return lax.ppermute(block, axis, route)  12.4 us
    dot_general x1, matrix products, per_device(): jnp.dot(gathered, flat_piece, preferred_element_type=jnp.float32)  10.6 us
  transfers between devices with their start and end apart: 6, of which 4 were waited for; matrix products, arithmetic and copies ran while one was open for 4% of the time, Pallas kernels for 0%

commit v1 on v0

--- a/solution.py
+++ b/solution.py
@@ -61,7 +61,10 @@
     scale = lax.rsqrt(squares / (chan_width * lax.axis_size("tp")) + norm_eps)
     my_gain = lax.dynamic_slice_in_dim(gain_full, lax.axis_index("tp") * chan_width, chan_width, 0)
     normed = (stream * scale[:, None] * my_gain).astype(jnp.bfloat16)
-    gathered = lax.all_gather(normed, "tp", axis=1, tiled=True)
+    gathered = jnp.concatenate(
+        lax.all_to_all(jnp.stack([normed for _ in range(lax.axis_size("tp"))], axis=0), "tp", 0, 0),
+        axis=1,
+    )
     piece = lax.all_gather(w_in, "seq", axis=0, tiled=True)
     flat_piece = piece.reshape(piece.shape[0], 3 * chan_width)
     proj = jnp.dot(gathered, flat_piece, preferred_element_type=jnp.float32).reshape(

time: 439 us -> 398 us (0.907); the launches traced: 438 us -> 390 us
  waiting for transfers between devices: 347 us -> 281 us
  local copies, waits for them, and re-layouts: 10.9 us -> 27 us
    all_gather x1 -> x0, waiting for transfers between devices: 81.6 us -> none  [per_device(): gathered = lax.all_gather(normed, 'tp', axis=1, tiled=True)]
    all_to_all x0 -> x1, waiting for transfers between devices: none -> 47.7 us  [per_device(): lax.all_to_all(jnp.stack([normed for _ in range(lax.axis_size('tp'))], ax...]
    all_gather x1, waiting for transfers between devices: 83.3 us -> 52.2 us  [per_device(): piece = lax.all_gather(w_in, 'seq', axis=0, tiled=True)]
    reshape x0 -> x2, local copies, waits for them, and re-layouts: none -> 13.9 us  [per_device(): jnp.concatenate(lax.all_to_all(jnp.stack([normed for _ in range(lax.axis_...]
    all_to_all x0 -> x1, starting transfers between devices: none -> 4.71 us  [per_device(): lax.all_to_all(jnp.stack([normed for _ in range(lax.axis_size('tp'))], ax...]
  transfers between devices with their start and end apart: 6 -> 6, of which waited for: 4 -> 4; matrix products, arithmetic and copies ran while one was open for 4% -> 9% of each run, Pallas kernels for 0% -> 0%
where the time goes in v1:
time: 398 us; the launch traced here: 390 us
  waiting for transfers between devices  281 us (71%)
  matrix products  28.3 us (7%)
  local copies, waits for them, and re-layouts  27 us (7%)
  blocking collectives  16.9 us (4%)
  starting transfers between devices  14.4 us (4%)
  between operations  13.3 us (3%)
  other arithmetic  9.27 us (2%)
    reduce_scatter x1, waiting for transfers between devices, per_device(): share = lax.psum_scatter(partial_out, 'tp', scatter_dimension=1, tiled=True)  116 us
    all_gather x1, waiting for transfers between devices, project_out(): lax.all_gather(w_out, 'seq', axis=1, tiled=True)  65.1 us
    all_gather x1, waiting for transfers between devices, per_device(): piece = lax.all_gather(w_in, 'seq', axis=0, tiled=True)  52.2 us
    all_to_all x1, waiting for transfers between devices, per_device(): lax.all_to_all(jnp.stack([normed for _ in range(lax.axis_size('tp'))], ax...  47.7 us
    psum x1, blocking collectives, per_device(): squares = lax.psum(jnp.sum(stream * stream, axis=1), 'tp')  16.9 us
    reshape x2, local copies, waits for them, and re-layouts, per_device(): jnp.concatenate(lax.all_to_all(jnp.stack([normed for _ in range(lax.axis_...  13.9 us
    dot_general x1, matrix products, per_device(): jnp.dot(gathered, flat_piece, preferred_element_type=jnp.float32)  10.6 us
    ppermute x2, starting transfers between devices, shifted(): return lax.ppermute(block, axis, route)  9.56 us
  transfers between devices with their start and end apart: 6, of which 4 were waited for; matrix products, arithmetic and copies ran while one was open for 9% of the time, Pallas kernels for 0%

profile of v1, /device:TPU:105, one launch (start us, length us, event | category | flops | bytes accessed | tf_op | source)
XLA Modules:
  0.0 390.4 jit_solution(17602491862667941647)
XLA Ops:
  6.5 0.0 copy-start
  6.5 0.0 all-gather.3.cloned.1.call-start
  6.5 0.7 all-gather.3.cloned.1.call-update
  7.3 0.0 reduce-scatter.2.cloned.1.call-start
  7.3 1.3 multiply_convert_fusion.1
  8.7 5.2 %collective-permute-start = (bf16[6,512]{1,0:T(8,128)(2,1)S(1)}, bf16[6,512]{1,0:T(8,128)(2,1)S(1)}, u32[]{:S(2)}, u32[]{:S(2)}) collective-permute-start(bf16[6,512]{1,0:T(8,128)(2,1)S(1)} %slice_bitcast_fusion.1), channel_id=1, source_target_pairs={{0,8},{8,16},{16,24},{24,32},{32,40},{40,48},{48,56},{56,64},{64,7... | collective-permute-start | bytes 18440 | tf_op jit(solution)/shard_map/ppermute | solution.py:15
  13.9 0.8 broadcast_in_dim.26
  14.6 0.1 reshape.83
  14.8 1.3 fusion.51
  16.1 0.7 convert_element_type.78
  16.8 0.0 collective-permute-done
  16.8 0.2 maximum_convert_fusion
  17.0 65.1 %all-gather.3.cloned.1.call-done = bf16[512,4096]{1,0:T(8,128)(2,1)} async-done(((bf16[512,128]{1,0:T(8,128)(2,1)}), bf16[512,4096]{1,0:T(8,128)(2,1)}) %all-gather.3.cloned.1.call-update) | async-done | bytes 4194320 | tf_op jit(solution)/shard_map/all_gather | solution.py:34
  82.0 8.7 %fusion.21 = f32[512,4096]{1,0:T(8,128)} fusion(bf16[512,4096]{1,0:T(8,128)(2,1)} %all-gather.3.cloned.1.call-done, f32[518,512]{1,0:T(8,128)S(1)} %maximum_convert_fusion, f32[512]{0:T(512)S(1)} %convert_element_type.78, f32[512]{0:T(512)S(1)} %bitcast.73, f32[512]{0:T(512)S(1)} %bitcast.74, f32[512]{0:T(512)S(1)} %bitcast.75, f32[512]{0:T(512)S(1)} %bitcast.76, ...), kind=kOutput, calls=%fused_computation.41 | convolution fusion | flops 2152464384 | bytes 20987904 | tf_op jit(solution)/shard_map/dot_general | solution.py:33
  90.7 0.0 copy-start.2
  90.7 0.0 copy-start.1
  90.7 0.0 reduce-scatter.2.cloned.1.call-update
  90.8 0.0 all-gather.5.cloned.1.call-start
  90.8 0.9 copy-done.2
  91.7 0.9 copy.32
  92.7 0.0 all-gather.5.cloned.1.call-update
  92.7 0.8 dynamic-slice_convert_fusion
  93.4 115.6 %reduce-scatter.2.cloned.1.call-done = f32[512,512]{1,0:T(8,128)} async-done(((f32[512,4096]{1,0:T(8,128)}), f32[512,512]{1,0:T(8,128)}) %reduce-scatter.2.cloned.1.call-update) | async-done | bytes 1048592 | tf_op jit(solution)/shard_map/reduce_scatter | solution.py:58
  209.1 0.0 copy-done.1
  209.1 1.4 multiply_reduce_fusion
  210.5 16.9 %psum.7 = f32[512]{0:T(512)S(1)} all-reduce(f32[512]{0:T(512)S(1)} %multiply_reduce_fusion), channel_id=1, replica_groups=mesh['seq'=32,'tp'=8] {'tp'}, use_global_device_ids=true, to_apply=%region_2.0 | all-reduce | flops 512 | bytes 4096 | tf_op jit(solution)/shard_map/psum | solution.py:60
  227.4 1.5 multiply_convert_fusion
  228.9 2.3 stack.2
  231.2 0.0 copy-start.3
  231.2 4.7 %all-to-all-start = ((bf16[8,512,512]{2,1,0:T(8,128)(2,1)}), bf16[8,512,512]{2,1,0:T(8,128)(2,1)}, u32[]{:S(2)}, u32[]{:S(2)}) async-start(bf16[8,512,512]{2,1,0:T(8,128)(2,1)} %stack.2), calls=%async_computation.1 | async-start | bytes 8388608 | tf_op jit(solution)/shard_map/all_to_all | solution.py:65
  235.9 0.0 copy-done.3
  236.0 0.0 copy-done
  236.0 3.3 select_bitcast_fusion
  239.4 47.7 %all-to-all-done = bf16[8,512,512]{2,1,0:T(8,128)(2,1)} async-done(((bf16[8,512,512]{2,1,0:T(8,128)(2,1)}), bf16[8,512,512]{2,1,0:T(8,128)(2,1)}, u32[]{:S(2)}, u32[]{:S(2)}) %all-to-all-start) | async-done | bytes 4194336 | tf_op jit(solution)/shard_map/all_to_all | solution.py:65
  287.0 6.5 %copy.31 = bf16[512,8,512]{2,1,0:T(8,128)(2,1)} copy(bf16[512,8,512]{2,0,1:T(8,128)(2,1)} %bitcast.10) | data formatting | bytes 8388608 | tf_op jit(solution)/shard_map/reshape | solution.py:64
  293.5 7.4 %reshape.90 = bf16[512,4096,1]{1,0,2:T(8,128)(2,1)} reshape(bf16[512,8,512]{2,1,0:T(8,128)(2,1)} %copy.31) | data formatting | bytes 8388608 | tf_op jit(solution)/shard_map/reshape | solution.py:64
  300.9 52.2 %all-gather.5.cloned.1.call-done = bf16[4096,3,512]{0,2,1:T(8,128)(2,1)} async-done(((bf16[128,3,512]{0,2,1:T(8,128)(2,1)}), bf16[4096,3,512]{0,2,1:T(8,128)(2,1)}) %all-gather.5.cloned.1.call-update) | async-done | bytes 12582928 | tf_op jit(solution)/shard_map/all_gather | solution.py:68
  353.1 10.6 %fusion = f32[512,3,512]{0,2,1:T(8,128)S(1)} fusion(bf16[512,4096,1]{1,0,2:T(8,128)(2,1)} %reshape.90, bf16[4096,3,512]{0,2,1:T(8,128)(2,1)} %all-gather.5.cloned.1.call-done), kind=kOutput, calls=%fused_computation | convolution fusion | flops 6442450944 | bytes 19922944 | tf_op jit(solution)/shard_map/dot_general | solution.py:70
  363.7 0.9 fusion.8
  364.6 0.0 slice-start
  364.6 2.1 convert_element_type.84
  366.7 1.6 slice.121
  368.2 4.4 %collective-permute-start.1 = (bf16[128,32,16]{0,2,1:T(8,128)(2,1)}, bf16[128,32,16]{0,2,1:T(8,128)(2,1)}, u32[]{:S(2)}, u32[]{:S(2)}) collective-permute-start(bf16[128,32,16]{0,2,1:T(8,128)(2,1)} %bitcast.18), channel_id=1, source_target_pairs={{0,8},{8,16},{16,24},{24,32},{32,40},{40,48},{48,56},{56,64},{64,7... | collective-permute-start | bytes 393224 | tf_op jit(solution)/shard_map/ppermute | solution.py:15
  372.6 3.2 fusion.19
  375.8 0.0 slice-done
  375.8 0.9 slice.102
  376.7 1.1 copy.35
  377.8 0.0 collective-permute-done.1
  377.8 2.5 fusion.5
  380.3 0.4 copy.37
  380.8 1.0 fusion.7
  381.8 2.0 copy.38
  (6 shorter events, 0.1 us)
Async XLA Ops:
  6.5 229.5 %copy-start = (bf16[32,128]{1,0:T(8,128)(2,1)S(1)}, bf16[32,128]{1,0:T(8,128)(2,1)}, u32[]{:S(2)}) copy-start(bf16[32,128]{1,0:T(8,128)(2,1)} %param.16) | copy-start | bytes 24580
  6.5 75.5 %all-gather.3.cloned.1.call-start = ((), (), s32[]{:S(2)}) async-start(), calls=%async_computation.2 | async-start | bytes 4325376 | tf_op jit(solution)/shard_map/all_gather | solution.py:34
  7.3 201.8 %reduce-scatter.2.cloned.1.call-start = ((), (), s32[]{:S(2)}) async-start(), calls=%async_computation.3 | async-start | bytes 9437184 | tf_op jit(solution)/shard_map/reduce_scatter | solution.py:58
  8.7 8.1 %collective-permute-start = (bf16[6,512]{1,0:T(8,128)(2,1)S(1)}, bf16[6,512]{1,0:T(8,128)(2,1)S(1)}, u32[]{:S(2)}, u32[]{:S(2)}) collective-permute-start(bf16[6,512]{1,0:T(8,128)(2,1)S(1)} %slice_bitcast_fusion.1), channel_id=1, source_target_pairs={{0,8},{8,16},{16,24},{24,32},{32,40},{40,48},{48,56},{56,64},{64,7... | collective-permute-start | bytes 18440 | tf_op jit(solution)/shard_map/ppermute | solution.py:15
  90.7 1.0 copy-start.2
  90.7 118.3 %copy-start.1 = (bf16[512,512]{1,0:T(8,128)(2,1)S(1)}, bf16[512,512]{1,0:T(8,128)(2,1)}, u32[]{:S(2)}) copy-start(bf16[512,512]{1,0:T(8,128)(2,1)} %param.10) | copy-start | bytes 1572868
  90.8 262.3 %all-gather.5.cloned.1.call-start = ((), (), s32[]{:S(2)}) async-start(), calls=%async_computation.4 | async-start | bytes 12976128 | tf_op jit(solution)/shard_map/all_gather | solution.py:68
  231.2 4.7 %copy-start.3 = (bf16[512]{0:T(512)(128)(2,1)S(1)}, bf16[512]{0:T(512)(128)(2,1)}, u32[]{:S(2)}) copy-start(bf16[512]{0:T(512)(128)(2,1)} %param.17) | copy-start | bytes 3076
  231.2 55.8 %all-to-all-start = ((bf16[8,512,512]{2,1,0:T(8,128)(2,1)}), bf16[8,512,512]{2,1,0:T(8,128)(2,1)}, u32[]{:S(2)}, u32[]{:S(2)}) async-start(bf16[8,512,512]{2,1,0:T(8,128)(2,1)} %stack.2), calls=%async_computation.1 | async-start | bytes 8388608 | tf_op jit(solution)/shard_map/all_to_all | solution.py:65
  364.6 11.2 %slice-start = ((bf16[512,1,512]{0,2,1:T(8,128)(2,1)}), bf16[384,1,512]{0,2,1:T(8,128)(2,1)S(1)}, s32[]{:S(2)}) async-start(bf16[512,1,512]{0,2,1:T(8,128)(2,1)} %fusion.8), calls=%async_computation.5 | async-start | bytes 786432 | tf_op jit(solution)/shard_map/slice | solution.py:80
  368.2 9.6 %collective-permute-start.1 = (bf16[128,32,16]{0,2,1:T(8,128)(2,1)}, bf16[128,32,16]{0,2,1:T(8,128)(2,1)}, u32[]{:S(2)}, u32[]{:S(2)}) collective-permute-start(bf16[128,32,16]{0,2,1:T(8,128)(2,1)} %bitcast.18), channel_id=1, source_target_pairs={{0,8},{8,16},{16,24},{24,32},{32,40},{40,48},{48,56},{56,64},{64,7... | collective-permute-start | bytes 393224 | tf_op jit(solution)/shard_map/ppermute | solution.py:15
Sparse Core Ops, SparseCore 0:
  9.1 72.8 all-gather.2
  90.9 118.1 reduce-scatter.1
  210.8 142.1 all-gather.4
